TPU v7x, 32 devices: a whole 2x2x4 slice. The times are simulated.
32 devices in a mesh: rot: 16 (over z, x, core), term: 2 (over y).
Axes of the slice: x: 2, y: 2, z: 4, core: 2. Of those that a mesh axis runs over, the one named last changes fastest.
Arguments:
- receptor_grids: bfloat16 [22, 128, 1024], P('term', 'rot'), may hold values from -6 to 6
- term_weights: float32 [22], P('term'), may hold values from 0.5 to 2
- atom_weights: float32 [22, 256], P('term'), may hold values from -0.125 to 0.125
- ligand_cells: int32 [3, 32, 256], P(None, 'rot'), may hold values from 0 to 15
Outputs:
- best_scores: float32 [4, 32], P(None, 'rot')
- best_overall: float32 [4], replicated
All inputs are finite; a program needn't handle non-finite values.
Results may differ from a plain program's by a relative error of at most 0.0017.
Values may be sent and summed in bfloat16 or wider, within the bound.
No kernel may reach another device: no remote copies, remote signals or barrier semaphores. Data moves between devices by JAX's collectives and lax.ppermute only.
A program may use at most 128 MiB of HBM per device.

v0:
```python
import math
import numpy as np
import jax
import jax.numpy as jnp
from jax import lax
from jax.sharding import PartitionSpec as P

G = 32
HZ = G // 2 + 1
LB = 16
HIGH = lax.Precision.HIGH
HIGHEST = lax.Precision.HIGHEST


def line_table(freq_count, cell_count):
    freq = np.arange(freq_count)[:, None]
    cell = np.arange(cell_count)[None, :]
    phase = (freq * cell % G).astype(np.float64) * (2.0 * math.pi / G)
    return (np.cos(phase).astype(np.float32), np.sin(phase).astype(np.float32))


def plane_tables(side):
    cy, sy = line_table(G, side)
    cz, sz = line_table(HZ, side)
    cy = jnp.asarray(cy.T)[:, None, :, None]
    sy = jnp.asarray(sy.T)[:, None, :, None]
    cz = jnp.asarray(cz.T)[None, :, None, :]
    sz = jnp.asarray(sz.T)[None, :, None, :]
    cos_t = (cy * cz - sy * sz).reshape(side * side, G * HZ)
    sin_t = (sy * cz + cy * sz).reshape(side * side, G * HZ)
    return (cos_t, sin_t)


def split_bf16(table):
    upper = table.astype(jnp.bfloat16)
    lower = (table - upper.astype(jnp.float32)).astype(jnp.bfloat16)
    return (upper, lower)


def mix_table(cell_count):
    cos_x, sin_x = line_table(G, cell_count)
    return jnp.asarray(np.concatenate([cos_x, sin_x], axis=0))


def dot2(rows, upper, lower):
    first = jnp.dot(rows, upper, preferred_element_type=jnp.float32)
    second = jnp.dot(rows, lower, preferred_element_type=jnp.float32)
    return first + second


def receptor_spectra(grids, cos_hi, cos_lo, sin_hi, sin_lo):
    terms, rows, cells = grids.shape
    receptors = rows // G
    flat = grids.reshape(terms * rows, cells)
    plane_re = dot2(flat, cos_hi, cos_lo).reshape(terms, receptors, G, G * HZ)
    plane_ims = dot2(flat, sin_hi, sin_lo).reshape(terms, receptors, G, G * HZ)
    mix = mix_table(G)
    mixed_re = jnp.einsum("px,trxq->trpq", mix, plane_re, precision=HIGH)
    mixed_ims = jnp.einsum("px,trxq->trpq", mix, plane_ims, precision=HIGH)
    spec_re = mixed_re[:, :, :G] - mixed_ims[:, :, G:]
    spec_im = -mixed_ims[:, :, :G] - mixed_re[:, :, G:]
    return (spec_re, spec_im)


def ligand_spectra(voxels, coefficients, box_cos, box_sin):
    rot_count = voxels.shape[1]
    terms = coefficients.shape[0]
    flat_index = (voxels[0] * LB + voxels[1]) * LB + voxels[2]
    cells = jnp.arange(LB**3, dtype=jnp.int32)
    onehot = (flat_index[:, :, None] == cells[None, None, :]).astype(jnp.float32)
    grid = jnp.einsum("ta,nac->tnc", coefficients, onehot, precision=HIGHEST)
    grid = grid.reshape(terms, rot_count, LB, LB * LB)
    plane_re = jnp.einsum("tnxc,cq->tnxq", grid, box_cos, precision=HIGH)
    plane_ims = jnp.einsum("tnxc,cq->tnxq", grid, box_sin, precision=HIGH)
    mix = mix_table(LB)
    mixed_re = jnp.einsum("px,tnxq->tnpq", mix, plane_re, precision=HIGH)
    mixed_ims = jnp.einsum("px,tnxq->tnpq", mix, plane_ims, precision=HIGH)
    lig_re = mixed_re[:, :, :G] - mixed_ims[:, :, G:]
    lig_im = -mixed_ims[:, :, :G] - mixed_re[:, :, G:]
    return (lig_re, lig_im)


def correlate(lig_re, lig_im, rec_re, rec_im):
    lr = lig_re[:, None]
    li = lig_im[:, None]
    rr = rec_re[:, :, None]
    ri = rec_im[:, :, None]
    prod_re = jnp.sum(lr * rr + li * ri, axis=0)
    prod_im = jnp.sum(lr * ri - li * rr, axis=0)
    return jnp.stack([prod_re, prod_im], axis=0)


def inverse_scores(products, cos_t, sin_t):
    mix = mix_table(G)
    mixed = jnp.einsum("xp,srnpq->srnxq", mix, products, precision=HIGH)
    inv_re = mixed[0, :, :, :G] - mixed[1, :, :, G:]
    inv_im = mixed[1, :, :, :G] + mixed[0, :, :, G:]
    freq_z = np.arange(G * HZ) % HZ
    fold = np.where((freq_z == 0) | (freq_z == G // 2), 1.0, 2.0) / float(G**3)
    fold = jnp.asarray(fold.astype(np.float32))
    scores = jnp.einsum("rnxq,cq->rnxc", inv_re * fold, cos_t, precision=HIGH)
    scores = scores - jnp.einsum("rnxq,cq->rnxc", inv_im * fold, sin_t, precision=HIGH)
    return scores


def body(receptor_grids, term_weights, atom_weights, ligand_cells):
    gathered = lax.all_gather(receptor_grids, "rot", axis=1, tiled=True)
    with jax.named_scope("twiddle_tables"):
        cos_t, sin_t = plane_tables(G)
        box_cos, box_sin = plane_tables(LB)
        cos_hi, cos_lo = split_bf16(cos_t)
        sin_hi, sin_lo = split_bf16(sin_t)
        tables = lax.optimization_barrier(
            (cos_t, sin_t, box_cos, box_sin, cos_hi, cos_lo, sin_hi, sin_lo)
        )
        cos_t, sin_t, box_cos, box_sin, cos_hi, cos_lo, sin_hi, sin_lo = tables
    with jax.named_scope("ligand_spectra"):
        coefficients = atom_weights * term_weights[:, None]
        lig_re, lig_im = ligand_spectra(ligand_cells, coefficients, box_cos, box_sin)
    with jax.named_scope("receptor_spectra"):
        rec_re, rec_im = receptor_spectra(gathered, cos_hi, cos_lo, sin_hi, sin_lo)
    with jax.named_scope("correlate"):
        products = correlate(lig_re, lig_im, rec_re, rec_im)
    products = lax.psum_scatter(products, "term", scatter_dimension=2, tiled=True)
    with jax.named_scope("inverse_scores"):
        scores = inverse_scores(products, cos_t, sin_t)
        best_here = jnp.max(scores, axis=(2, 3))
    best_all = lax.all_gather(best_here, ("rot", "term"), axis=1, tiled=True)
    rot_local = ligand_cells.shape[1]
    start = lax.axis_index("rot") * rot_local
    best_scores = lax.dynamic_slice_in_dim(best_all, start, rot_local, axis=1)
    best_overall = jnp.max(best_all, axis=1)
    return (best_scores, best_overall)


def solution(mesh):
    placed = (P("term", "rot", None), P("term"), P("term", None), P(None, "rot", None))
    return jax.shard_map(
        body, mesh=mesh, in_specs=placed, out_specs=(P(None, "rot"), P()), check_vma=False
    )
```

profile of v0, /device:TPU:0, one launch (start us, length us, event | category | flops | bytes accessed | tf_op | source)
XLA Modules:
  0.0 238.6 jit_solution(8877241703728081015)
XLA Ops:
  7.2 0.0 all-gather.3.cloned.1.call-start
  7.2 0.7 all-gather.3.cloned.1.call-update
  7.9 0.0 all-reduce.3.cloned.1.call-start
  7.9 8.2 %multiply_add_fusion = (f32[32,32,32,17]{1,0,3,2:T(8,128)}, f32[32,32,32,17]{1,0,3,2:T(8,128)}) fusion(f32[32,17]{0,1:T(8,128)} %constant.43.clone, f32[32,32]{0,1:T(8,128)} %constant.41.clone, f32[32,17]{0,1:T(8,128)} %constant.42.clone, f32[32,32]{0,1:T(8,128)} %constant.40.clone), kind=kLoop, calls=%fused_computation | loop fusion | flops 3342336 | bytes 4468992 | tf_op jit(solution)/shard_map/twiddle_tables/add | solution.py:30
  16.2 7.0 %add.65 = f32[1024,544]{0,1:T(8,128)S(1)} reshape(f32[32,32,32,17]{1,0,3,2:T(8,128)} %get-tuple-element.28) | data formatting | bytes 4456448 | tf_op jit(solution)/shard_map/twiddle_tables/add | solution.py:30
  23.2 0.0 copy-start.9
  23.2 0.0 copy-start.10
  23.2 0.0 copy-start.11
  23.2 0.0 copy-start.12
  23.2 7.9 %sub.49 = f32[1024,544]{0,1:T(8,128)} reshape(f32[32,32,32,17]{1,0,3,2:T(8,128)} %get-tuple-element.29) | data formatting | bytes 4456448 | tf_op jit(solution)/shard_map/twiddle_tables/sub | solution.py:29
  31.1 0.0 copy-done.10
  31.2 4.5 %multiply_add_fusion.1 = (f32[16,16,32,17]{3,2,1,0:T(8,128)}, f32[16,16,32,17]{3,2,1,0:T(8,128)}) fusion(f32[16,17]{1,0:T(8,128)S(1)} %copy-done.12, f32[16,32]{1,0:T(8,128)S(1)} %copy-done.10, f32[16,17]{1,0:T(8,128)S(1)} %copy-done.11, f32[16,32]{1,0:T(8,128)S(1)} %copy-done.9), kind=kLoop, calls=%fused_computation.6 | loop fusion | flops 835584 | bytes 1120384 | tf_op jit(solution)/shard_map/twiddle_tables/add | solution.py:30
  35.7 4.5 %add.67 = f32[256,544]{1,0:T(8,128)S(1)} reshape(f32[16,16,32,17]{3,2,1,0:T(8,128)} %get-tuple-element.30) | data formatting | bytes 1114112 | tf_op jit(solution)/shard_map/twiddle_tables/add | solution.py:30
  40.1 5.1 %sub.51 = f32[256,544]{1,0:T(8,128)} reshape(f32[16,16,32,17]{3,2,1,0:T(8,128)} %get-tuple-element.31) | data formatting | bytes 1114112 | tf_op jit(solution)/shard_map/twiddle_tables/sub | solution.py:29
  45.3 5.1 %subtract_convert_fusion = (bf16[1024,544]{0,1:T(8,128)(2,1)}, bf16[1024,544]{0,1:T(8,128)(2,1)}, bf16[1024,544]{0,1:T(8,128)(2,1)}, bf16[1024,544]{0,1:T(8,128)(2,1)}) fusion(f32[1024,544]{0,1:T(8,128)S(1)} %add.65, f32[1024,544]{0,1:T(8,128)} %sub.49), kind=kLoop, calls=%fused_computation.22 | loop fusion | flops 4456448 | bytes 8912896 | tf_op jit(solution)/shard_map/twiddle_tables/convert_element_type | solution.py:36
  50.4 0.0 copy-start.7
  50.4 3.6 %fusion = f32[11,2,4096]{2,0,1:T(8,128)} fusion(s32[2,256]{1,0:T(2,128)S(1)} %add_bitcast_fusion, f32[11,256]{1,0:T(8,128)S(1)} %copy-done.16, f32[11]{0:T(128)S(1)} %copy-done.17), kind=kOutput, calls=%fused_computation.3 | convolution fusion | flops 278924032 | bytes 373804 | tf_op jit(solution)/shard_map/ligand_spectra/ta,nac->tnc/dot_general | solution.py:71
  54.0 1.1 reshape.132
  55.2 0.6 fusion.15
  55.8 1.7 fusion.17
  57.5 1.6 convolution_bitcast_fusion.2
  59.1 1.6 convolution_bitcast_fusion.3
  60.7 0.0 copy-start.5
  60.7 2.3 slice_subtract_fusion.3
  63.1 3.9 %fusion.35 = f32[544,1408]{1,0:T(8,128)S(1)} fusion(bf16[1024,544]{0,1:T(8,128)(2,1)S(1)} %copy-done.5, bf16[1408,1024]{1,0:T(8,128)(2,1)} %bitcast.113), kind=kOutput, calls=%fused_computation.56 | convolution fusion | flops 1568669696 | bytes 7061504 | tf_op jit(solution)/shard_map/receptor_spectra/dot_general | solution.py:46
  67.0 3.6 %fusion.3 = f32[1408,544]{0,1:T(8,128)} fusion(f32[544,1408]{1,0:T(8,128)S(1)} %fusion.35, bf16[1024,544]{0,1:T(8,128)(2,1)S(1)} %copy-done.4, bf16[1408,1024]{1,0:T(8,128)(2,1)S(1)} %bitcast.115), kind=kOutput, calls=%fused_computation.15 | convolution fusion | flops 1569435648 | bytes 10125312 | tf_op jit(solution)/shard_map/receptor_spectra/dot_general | solution.py:47
  70.6 4.9 %copy.44 = f32[1408,544]{1,0:T(8,128)} copy(f32[1408,544]{0,1:T(8,128)} %fusion.3) | data formatting | bytes 6127616 | tf_op jit(solution)/shard_map/receptor_spectra/add | solution.py:48
  75.5 3.9 %fusion.36 = f32[544,1408]{1,0:T(8,128)S(1)} fusion(bf16[1024,544]{0,1:T(8,128)(2,1)S(1)} %copy-done.3, bf16[1408,1024]{1,0:T(8,128)(2,1)} %bitcast.114), kind=kOutput, calls=%fused_computation.57 | convolution fusion | flops 1568669696 | bytes 7061504 | tf_op jit(solution)/shard_map/receptor_spectra/dot_general | solution.py:46
  79.4 3.6 %fusion.2 = f32[1408,544]{0,1:T(8,128)} fusion(f32[544,1408]{1,0:T(8,128)S(1)} %fusion.36, bf16[1024,544]{0,1:T(8,128)(2,1)S(1)} %copy-done.2, bf16[1408,1024]{1,0:T(8,128)(2,1)S(1)} %bitcast.116), kind=kOutput, calls=%fused_computation.13 | convolution fusion | flops 1569435648 | bytes 10125312 | tf_op jit(solution)/shard_map/receptor_spectra/dot_general | solution.py:47
  83.0 4.8 %copy.45 = f32[1408,544]{1,0:T(8,128)} copy(f32[1408,544]{0,1:T(8,128)} %fusion.2) | data formatting | bytes 6127616 | tf_op jit(solution)/shard_map/receptor_spectra/add | solution.py:48
  87.9 0.0 copy-done.6
  87.9 5.2 %convolution_bitcast_fusion.1 = f32[11,4,64,544]{3,2,1,0:T(8,128)S(1)} fusion(f32[11,4,32,544]{3,2,1,0:T(8,128)} %bitcast.105, f32[64,32,1,1]{0,1,3,2:T(8,128)S(1)} %copy-done.6), kind=kOutput, calls=%fused_computation.17 | convolution fusion | flops 294125568 | bytes 9199616 | tf_op jit(solution)/shard_map/receptor_spectra/px,trxq->trpq/dot_general | solution.py:58
  93.1 5.1 %convolution_bitcast_fusion = f32[11,4,64,544]{3,2,1,0:T(8,128)} fusion(f32[11,4,32,544]{3,2,1,0:T(8,128)S(1)} %bitcast.106, f32[64,32,1,1]{0,1,3,2:T(8,128)S(1)} %copy-done.6), kind=kOutput, calls=%fused_computation.16 | convolution fusion | flops 294125568 | bytes 9199616 | tf_op jit(solution)/shard_map/receptor_spectra/px,trxq->trpq/dot_general | solution.py:59
  98.2 6.6 %slice_subtract_fusion.1 = (f32[11,4,32,544]{3,2,1,0:T(8,128)S(1)}, f32[11,4,32,544]{3,2,1,0:T(8,128)}) fusion(f32[11,4,64,544]{3,2,1,0:T(8,128)} %convolution_bitcast_fusion, f32[11,4,64,544]{3,2,1,0:T(8,128)S(1)} %convolution_bitcast_fusion.1), kind=kLoop, calls=%fused_computation.11 | loop fusion | flops 2297856 | bytes 18382848 | tf_op jit(solution)/shard_map/receptor_spectra/sub | solution.py:60
  104.8 4.6 %add_reduce_fusion = (f32[4,2,32,544]{3,2,1,0:T(8,128)S(1)}, f32[4,2,32,544]{3,2,1,0:T(8,128)S(1)}) fusion(f32[11,4,32,544]{3,2,1,0:T(8,128)} %get-tuple-element.25, f32[11,2,32,544]{3,2,1,0:T(8,128)} %get-tuple-element.27, f32[11,4,32,544]{3,2,1,0:T(8,128)S(1)} %get-tuple-element.24, f32[11,2,32,544]{3,2,1,0:T(8,128)} %get-tuple-element.26), kind=kLoop, calls=%fused_computation.5 | loop fusion | flops 11976704 | bytes 10305536 | tf_op jit(solution)/shard_map/correlate/reduce_sum | solution.py:88
  109.5 0.0 copy-start.18
  109.5 0.0 copy-start.8
  109.5 1.2 pad_maximum_fusion
  110.7 0.0 all-reduce.3.cloned.1.call-update
  110.7 0.6 dynamic-slice.2
  111.3 48.1 %all-reduce.3.cloned.1.call-done = f32[2,4,2,32,544]{4,3,2,1,0:T(8,128)} async-done(((f32[2,4,2,32,544]{4,3,2,1,0:T(8,128)}), f32[2,4,2,32,544]{4,3,2,1,0:T(8,128)}) %all-reduce.3.cloned.1.call-update) | async-done | bytes 1114128
  159.4 2.6 %fusion.14 = f32[2,4,544,64]{2,3,1,0:T(8,128)S(1)} fusion(f32[64,32,1,1]{0,1,3,2:T(8,128)S(1)} %copy-done.6, f32[2,4,2,32,544]{4,3,2,1,0:T(8,128)} %all-reduce.3.cloned.1.call-done, u32[]{:T(128)} %bitcast.40), kind=kOutput, calls=%fused_computation.33 | convolution fusion | flops 53477376 | bytes 1778176 | tf_op jit(solution)/shard_map/inverse_scores/xp,srnpq->srnxq/dot_general | solution.py:95
  162.0 0.9 fusion.4
  163.0 0.0 copy-done
  163.0 1.1 fusion.11
  164.1 66.6 %all-gather = f32[32,1,4]{2,1,0:T(1,128)S(1)} all-gather(f32[1,1,4]{2,1,0:T(1,128)S(1)} %bitcast.111), channel_id=1, replica_groups=mesh['rot'=16,'term'=2] {'rot','term'}, dimensions={0}, use_global_device_ids=true | all-gather | bytes 528 | tf_op jit(solution)/shard_map/all_gather | solution.py:128
  230.7 0.6 constant_dynamic-slice_fusion
  231.2 0.6 reduce_max.22
  (29 shorter events, 0.1 us)
Async XLA Ops:
  7.2 55.9 %all-gather.3.cloned.1.call-start = ((), (), s32[]{:S(2)}) async-start(), calls=%async_computation | async-start | bytes 3063808 | tf_op jit(solution)/shard_map/all_gather | solution.py:107
  7.9 151.5 %all-reduce.3.cloned.1.call-start = ((), (), s32[]{:S(2)}) async-start(), calls=%async_computation.1 | async-start | bytes 2621440
  23.2 8.0 %copy-start.9 = (f32[16,32]{1,0:T(8,128)S(1)}, f32[16,32]{1,0:T(8,128)}, u32[]{:S(2)}) copy-start(f32[16,32]{1,0:T(8,128)} %constant.44.clone) | copy-start | bytes 6148
  23.2 8.0 %copy-start.10 = (f32[16,32]{1,0:T(8,128)S(1)}, f32[16,32]{1,0:T(8,128)}, u32[]{:S(2)}) copy-start(f32[16,32]{1,0:T(8,128)} %constant.45.clone) | copy-start | bytes 6148
  23.2 7.9 %copy-start.11 = (f32[16,17]{1,0:T(8,128)S(1)}, f32[16,17]{1,0:T(8,128)}, u32[]{:S(2)}) copy-start(f32[16,17]{1,0:T(8,128)} %constant.46.clone) | copy-start | bytes 3268
  23.2 7.9 %copy-start.12 = (f32[16,17]{1,0:T(8,128)S(1)}, f32[16,17]{1,0:T(8,128)}, u32[]{:S(2)}) copy-start(f32[16,17]{1,0:T(8,128)} %constant.47.clone) | copy-start | bytes 3268
  45.3 5.1 %copy-start.13 = (s32[3,2,256]{2,1,0:T(2,128)S(1)}, s32[3,2,256]{2,1,0:T(2,128)}, u32[]{:S(2)}) copy-start(s32[3,2,256]{2,1,0:T(2,128)} %param.19) | copy-start | bytes 18436
  45.3 5.1 %copy-start.16 = (f32[11,256]{1,0:T(8,128)S(1)}, f32[11,256]{1,0:T(8,128)}, u32[]{:S(2)}) copy-start(f32[11,256]{1,0:T(8,128)} %param.18) | copy-start | bytes 33796
  45.3 5.2 %copy-start.17 = (f32[11]{0:T(128)S(1)}, f32[11]{0:T(128)}, u32[]{:S(2)}) copy-start(f32[11]{0:T(128)} %param.17) | copy-start | bytes 136
  50.4 7.1 %copy-start.7 = (f32[64,16,1,1]{0,1,3,2:T(8,128)S(1)}, f32[64,16,1,1]{0,1,3,2:T(8,128)}, u32[]{:S(2)}) copy-start(f32[64,16,1,1]{0,1,3,2:T(8,128)} %constant.60) | copy-start | bytes 12292
  60.7 2.3 copy-start.5
  63.1 3.9 %copy-start.4 = (bf16[1024,544]{0,1:T(8,128)(2,1)S(1)}, bf16[1024,544]{0,1:T(8,128)(2,1)}, u32[]{:S(2)}) copy-start(bf16[1024,544]{0,1:T(8,128)(2,1)} %get-tuple-element.13) | copy-start | bytes 3342340
  63.1 3.9 %copy-start.14 = (bf16[11,128,1024]{2,1,0:T(8,128)(2,1)S(1)}, bf16[11,128,1024]{2,1,0:T(8,128)(2,1)}, u32[]{:S(2)}) copy-start(bf16[11,128,1024]{2,1,0:T(8,128)(2,1)} %all-gather.3.cloned.1.call-done) | copy-start | bytes 8650756
  70.6 4.9 %copy-start.3 = (bf16[1024,544]{0,1:T(8,128)(2,1)S(1)}, bf16[1024,544]{0,1:T(8,128)(2,1)}, u32[]{:S(2)}) copy-start(bf16[1024,544]{0,1:T(8,128)(2,1)} %get-tuple-element.14) | copy-start | bytes 3342340
  75.5 3.9 %copy-start.2 = (bf16[1024,544]{0,1:T(8,128)(2,1)S(1)}, bf16[1024,544]{0,1:T(8,128)(2,1)}, u32[]{:S(2)}) copy-start(bf16[1024,544]{0,1:T(8,128)(2,1)} %get-tuple-element.15) | copy-start | bytes 3342340
  75.5 3.9 %copy-start.15 = (bf16[11,128,1024]{2,1,0:T(8,128)(2,1)S(1)}, bf16[11,128,1024]{2,1,0:T(8,128)(2,1)}, u32[]{:S(2)}) copy-start(bf16[11,128,1024]{2,1,0:T(8,128)(2,1)} %all-gather.3.cloned.1.call-done) | copy-start | bytes 8650756
  83.0 4.8 %copy-start.6 = (f32[64,32,1,1]{0,1,3,2:T(8,128)S(1)}, f32[64,32,1,1]{0,1,3,2:T(8,128)}, u32[]{:S(2)}) copy-start(f32[64,32,1,1]{0,1,3,2:T(8,128)} %constant.61) | copy-start | bytes 24580
  87.9 5.2 %copy-start.1 = (f32[1408,544]{1,0:T(8,128)S(1)}, f32[1408,544]{1,0:T(8,128)}, u32[]{:S(2)}) copy-start(f32[1408,544]{1,0:T(8,128)} %copy.45) | copy-start | bytes 9191428
  109.5 1.3 copy-start.18
  109.5 52.6 %copy-start.8 = (f32[544]{0:T(1024)S(1)}, f32[544]{0:T(1024)}, u32[]{:S(2)}) copy-start(f32[544]{0:T(1024)} %constant.50.clone) | copy-start | bytes 6532
  159.4 3.6 %copy-start = (f32[1024,544]{0,1:T(8,128)S(1)}, f32[1024,544]{0,1:T(8,128)}, u32[]{:S(2)}) copy-start(f32[1024,544]{0,1:T(8,128)} %sub.49) | copy-start | bytes 6684676
Sparse Core Ops, SparseCore 0:
  10.2 47.0 all-gather.2
  110.8 48.5 all-reduce.2
where the time goes:
time: 239 us
  blocking collectives  66.6 us (28%)
  waiting for transfers between devices  48.8 us (20%)
  matrix products  39.1 us (16%)
  local copies, waits for them, and re-layouts  36.6 us (15%)
  other arithmetic  33.2 us (14%)
  between operations  14.3 us (6%)
    all_gather x1, blocking collectives, body(): best_all = lax.all_gather(best_here, ('rot', 'term'), axis=1, tiled=True)  66.6 us
    unnamed x3, waiting for transfers between devices  48.8 us
    sub x2, local copies, waits for them, and re-layouts, plane_tables(): cos_t = (cy * cz - sy * sz).reshape(side * side, G * HZ)  13 us
    add x2, other arithmetic, plane_tables(): sin_t = (sy * cz + cy * sz).reshape(side * side, G * HZ)  12.7 us
    add x2, local copies, waits for them, and re-layouts, plane_tables(): sin_t = (sy * cz + cy * sz).reshape(side * side, G * HZ)  11.5 us
    add x2, local copies, waits for them, and re-layouts, dot2(): return first + second  9.7 us
    dot_general x2, matrix products, dot2(): first = jnp.dot(rows, upper, preferred_element_type=jnp.float32)  7.78 us
    dot_general x2, matrix products, dot2(): second = jnp.dot(rows, lower, preferred_element_type=jnp.float32)  7.23 us
  transfers between devices with their start and end apart: 2, of which 1 were waited for; matrix products, arithmetic and copies ran while one was open for 23% of the time, Pallas kernels for 0%

commit v1 on v0

--- a/solution.py
+++ b/solution.py
@@ -10,6 +10,29 @@
 LB = 16
 HIGH = lax.Precision.HIGH
 HIGHEST = lax.Precision.HIGHEST
+
+
+def joined_along(blocks, dim):
+    shape = list(blocks.shape[1:])
+    shape[dim] *= blocks.shape[0]
+    return jnp.moveaxis(blocks, 0, dim).reshape(shape)
+
+
+def collected_by_bits(value, axis):
+    peers, place = (lax.axis_size(axis), lax.axis_index(axis))
+    blocks, bit = (value[None], 1)
+    while bit < peers:
+        received = lax.ppermute(blocks, axis, [(i, i ^ bit) for i in range(peers)])
+        low = place & bit == 0
+        blocks = jnp.concatenate(
+            [jnp.where(low, blocks, received), jnp.where(low, received, blocks)]
+        )
+        bit *= 2
+    return blocks
+
+
+def collect(value, axis, dim):
+    return joined_along(collected_by_bits(value, axis), dim)
 
 
 def line_table(freq_count, cell_count):
@@ -125,7 +148,7 @@
     with jax.named_scope("inverse_scores"):
         scores = inverse_scores(products, cos_t, sin_t)
         best_here = jnp.max(scores, axis=(2, 3))
-    best_all = lax.all_gather(best_here, ("rot", "term"), axis=1, tiled=True)
+    best_all = collect(best_here, ("rot", "term"), 1)
     rot_local = ligand_cells.shape[1]
     start = lax.axis_index("rot") * rot_local
     best_scores = lax.dynamic_slice_in_dim(best_all, start, rot_local, axis=1)

time: 239 us -> 191 us (0.80)
  blocking collectives: 66.6 us -> 0 us
  waiting for transfers between devices: 48.8 us -> 59.5 us
  starting transfers between devices: 0.08 us -> 6 us
    all_gather x1 -> x0, blocking collectives: 66.6 us -> none  [body(): best_all = lax.all_gather(best_here, ('rot', 'term'), axis=1, tiled=True)]
    ppermute x0 -> x5, waiting for transfers between devices: none -> 10.7 us  [collected_by_bits(): received = lax.ppermute(blocks, axis, [(i, i ^ bit) for i in range(peers)])]
    ppermute x0 -> x5, starting transfers between devices: none -> 5.93 us  [collected_by_bits(): received = lax.ppermute(blocks, axis, [(i, i ^ bit) for i in range(peers)])]
  transfers between devices with their start and end apart: 2 -> 7, of which waited for: 1 -> 6; matrix products, arithmetic and copies ran while one was open for 23% -> 29% of each run, Pallas kernels for 0% -> 0%
where the time goes in v1:
time: 191 us
  waiting for transfers between devices  59.5 us (31%)
  matrix products  38.9 us (20%)
  local copies, waits for them, and re-layouts  36.9 us (19%)
  other arithmetic  35.3 us (18%)
  between operations  14.4 us (8%)
  starting transfers between devices  6 us (3%)
    unnamed x3, waiting for transfers between devices  48.8 us
    sub x2, local copies, waits for them, and re-layouts, plane_tables(): cos_t = (cy * cz - sy * sz).reshape(side * side, G * HZ)  13.1 us
    add x2, other arithmetic, plane_tables(): sin_t = (sy * cz + cy * sz).reshape(side * side, G * HZ)  12.8 us
    add x2, local copies, waits for them, and re-layouts, plane_tables(): sin_t = (sy * cz + cy * sz).reshape(side * side, G * HZ)  11.5 us
    ppermute x5, waiting for transfers between devices, collected_by_bits(): received = lax.ppermute(blocks, axis, [(i, i ^ bit) for i in range(peers)])  10.7 us
    add x2, local copies, waits for them, and re-layouts, dot2(): return first + second  9.67 us
    dot_general x2, matrix products, dot2(): first = jnp.dot(rows, upper, preferred_element_type=jnp.float32)  7.78 us
    sub x1, other arithmetic, receptor_spectra(): spec_re = mixed_re[:, :, :G] - mixed_ims[:, :, G:]  7.76 us
  transfers between devices with their start and end apart: 7, of which 6 were waited for; matrix products, arithmetic and copies ran while one was open for 29% of the time, Pallas kernels for 0%

profile of v1, /device:TPU:0, one launch (start us, length us, event | category | flops | bytes accessed | tf_op | source)
XLA Modules:
  0.0 190.9 jit_solution(16604146344426126184)
XLA Ops:
  7.2 0.7 all-gather.2.cloned.1.call-update
  7.9 8.3 %multiply_add_fusion = (f32[32,32,32,17]{1,0,3,2:T(8,128)}, f32[32,32,32,17]{1,0,3,2:T(8,128)}) fusion(f32[32,17]{0,1:T(8,128)} %constant.53.clone, f32[32,32]{0,1:T(8,128)} %constant.51.clone, f32[32,17]{0,1:T(8,128)} %constant.52.clone, f32[32,32]{0,1:T(8,128)} %constant.50.clone), kind=kLoop, calls=%fused_computation | loop fusion | flops 3342336 | bytes 4468992 | tf_op jit(solution)/shard_map/twiddle_tables/add | solution.py:53
  16.2 7.0 %add.69 = f32[1024,544]{0,1:T(8,128)S(1)} reshape(f32[32,32,32,17]{1,0,3,2:T(8,128)} %get-tuple-element.32) | data formatting | bytes 4456448 | tf_op jit(solution)/shard_map/twiddle_tables/add | solution.py:53
  23.3 7.9 %sub.49 = f32[1024,544]{0,1:T(8,128)} reshape(f32[32,32,32,17]{1,0,3,2:T(8,128)} %get-tuple-element.33) | data formatting | bytes 4456448 | tf_op jit(solution)/shard_map/twiddle_tables/sub | solution.py:52
  31.3 4.5 %multiply_add_fusion.1 = (f32[16,16,32,17]{3,2,1,0:T(8,128)}, f32[16,16,32,17]{3,2,1,0:T(8,128)}) fusion(f32[16,17]{1,0:T(8,128)S(1)} %copy-done.13, f32[16,32]{1,0:T(8,128)S(1)} %copy-done.11, f32[16,17]{1,0:T(8,128)S(1)} %copy-done.12, f32[16,32]{1,0:T(8,128)S(1)} %copy-done.10), kind=kLoop, calls=%fused_computation.6 | loop fusion | flops 835584 | bytes 1120384 | tf_op jit(solution)/shard_map/twiddle_tables/add | solution.py:53
  35.8 4.5 %add.71 = f32[256,544]{1,0:T(8,128)S(1)} reshape(f32[16,16,32,17]{3,2,1,0:T(8,128)} %get-tuple-element.34) | data formatting | bytes 1114112 | tf_op jit(solution)/shard_map/twiddle_tables/add | solution.py:53
  40.3 5.1 %sub.51 = f32[256,544]{1,0:T(8,128)} reshape(f32[16,16,32,17]{3,2,1,0:T(8,128)} %get-tuple-element.35) | data formatting | bytes 1114112 | tf_op jit(solution)/shard_map/twiddle_tables/sub | solution.py:52
  45.4 5.1 %subtract_convert_fusion = (bf16[1024,544]{0,1:T(8,128)(2,1)}, bf16[1024,544]{0,1:T(8,128)(2,1)}, bf16[1024,544]{0,1:T(8,128)(2,1)}, bf16[1024,544]{0,1:T(8,128)(2,1)}) fusion(f32[1024,544]{0,1:T(8,128)S(1)} %add.69, f32[1024,544]{0,1:T(8,128)} %sub.49), kind=kLoop, calls=%fused_computation.22 | loop fusion | flops 4456448 | bytes 8912896 | tf_op jit(solution)/shard_map/twiddle_tables/convert_element_type | solution.py:59
  50.5 3.6 %fusion = f32[11,2,4096]{2,0,1:T(8,128)} fusion(s32[2,256]{1,0:T(2,128)S(1)} %add_bitcast_fusion, f32[11,256]{1,0:T(8,128)S(1)} %copy-done.17, f32[11]{0:T(128)S(1)} %copy-done.18), kind=kOutput, calls=%fused_computation.3 | convolution fusion | flops 278924032 | bytes 373804 | tf_op jit(solution)/shard_map/ligand_spectra/ta,nac->tnc/dot_general | solution.py:94
  54.1 1.1 reshape.129
  55.3 0.6 fusion.15
  55.9 1.7 fusion.17
  57.6 1.6 convolution_bitcast_fusion.2
  59.2 1.6 convolution_bitcast_fusion.3
  60.9 2.4 %slice_subtract_fusion.3 = (f32[11,2,32,544]{3,2,1,0:T(8,128)}, f32[11,2,32,544]{3,2,1,0:T(8,128)}) fusion(f32[11,2,64,544]{3,2,1,0:T(8,128)S(1)} %convolution_bitcast_fusion.2, f32[11,2,64,544]{3,2,1,0:T(8,128)S(1)} %convolution_bitcast_fusion.3), kind=kLoop, calls=%fused_computation.28 | loop fusion | flops 1148928 | bytes 9191424 | tf_op jit(solution)/shard_map/ligand_spectra/sub | solution.py:101
  63.3 3.9 %fusion.37 = f32[544,1408]{1,0:T(8,128)S(1)} fusion(bf16[1024,544]{0,1:T(8,128)(2,1)S(1)} %copy-done.6, bf16[1408,1024]{1,0:T(8,128)(2,1)} %bitcast.115), kind=kOutput, calls=%fused_computation.73 | convolution fusion | flops 1568669696 | bytes 7061504 | tf_op jit(solution)/shard_map/receptor_spectra/dot_general | solution.py:69
  67.2 3.5 %fusion.3 = f32[1408,544]{0,1:T(8,128)} fusion(f32[544,1408]{1,0:T(8,128)S(1)} %fusion.37, bf16[1024,544]{0,1:T(8,128)(2,1)S(1)} %copy-done.5, bf16[1408,1024]{1,0:T(8,128)(2,1)S(1)} %bitcast.117), kind=kOutput, calls=%fused_computation.15 | convolution fusion | flops 1569435648 | bytes 10125312 | tf_op jit(solution)/shard_map/receptor_spectra/dot_general | solution.py:70
  70.7 4.9 %copy.50 = f32[1408,544]{1,0:T(8,128)} copy(f32[1408,544]{0,1:T(8,128)} %fusion.3) | data formatting | bytes 6127616 | tf_op jit(solution)/shard_map/receptor_spectra/add | solution.py:71
  75.6 3.9 %fusion.38 = f32[544,1408]{1,0:T(8,128)S(1)} fusion(bf16[1024,544]{0,1:T(8,128)(2,1)S(1)} %copy-done.4, bf16[1408,1024]{1,0:T(8,128)(2,1)} %bitcast.116), kind=kOutput, calls=%fused_computation.74 | convolution fusion | flops 1568669696 | bytes 7061504 | tf_op jit(solution)/shard_map/receptor_spectra/dot_general | solution.py:69
  79.5 3.5 %fusion.2 = f32[1408,544]{0,1:T(8,128)} fusion(f32[544,1408]{1,0:T(8,128)S(1)} %fusion.38, bf16[1024,544]{0,1:T(8,128)(2,1)S(1)} %copy-done.3, bf16[1408,1024]{1,0:T(8,128)(2,1)S(1)} %bitcast.118), kind=kOutput, calls=%fused_computation.13 | convolution fusion | flops 1569435648 | bytes 10125312 | tf_op jit(solution)/shard_map/receptor_spectra/dot_general | solution.py:70
  83.1 4.8 %copy.51 = f32[1408,544]{1,0:T(8,128)} copy(f32[1408,544]{0,1:T(8,128)} %fusion.2) | data formatting | bytes 6127616 | tf_op jit(solution)/shard_map/receptor_spectra/add | solution.py:71
  87.9 5.2 %convolution_bitcast_fusion.1 = f32[11,4,64,544]{3,2,1,0:T(8,128)S(1)} fusion(f32[11,4,32,544]{3,2,1,0:T(8,128)} %bitcast.107, f32[64,32,1,1]{0,1,3,2:T(8,128)S(1)} %copy-done.7), kind=kOutput, calls=%fused_computation.17 | convolution fusion | flops 294125568 | bytes 9199616 | tf_op jit(solution)/shard_map/receptor_spectra/px,trxq->trpq/dot_general | solution.py:81
  93.1 5.0 %convolution_bitcast_fusion = f32[11,4,64,544]{3,2,1,0:T(8,128)} fusion(f32[11,4,32,544]{3,2,1,0:T(8,128)S(1)} %bitcast.108, f32[64,32,1,1]{0,1,3,2:T(8,128)S(1)} %copy-done.7), kind=kOutput, calls=%fused_computation.16 | convolution fusion | flops 294125568 | bytes 9199616 | tf_op jit(solution)/shard_map/receptor_spectra/px,trxq->trpq/dot_general | solution.py:82
  98.1 7.8 %slice_subtract_fusion.1 = (f32[11,4,32,544]{3,2,1,0:T(8,128)}, f32[11,4,32,544]{3,2,1,0:T(8,128)}) fusion(f32[11,4,64,544]{3,2,1,0:T(8,128)} %convolution_bitcast_fusion, f32[11,4,64,544]{3,2,1,0:T(8,128)S(1)} %convolution_bitcast_fusion.1), kind=kLoop, calls=%fused_computation.11 | loop fusion | flops 2297856 | bytes 18382848 | tf_op jit(solution)/shard_map/receptor_spectra/sub | solution.py:83
  105.9 5.1 %add_reduce_fusion = (f32[4,2,32,544]{3,2,1,0:T(8,128)S(1)}, f32[4,2,32,544]{3,2,1,0:T(8,128)S(1)}) fusion(f32[11,4,32,544]{3,2,1,0:T(8,128)} %get-tuple-element.29, f32[11,2,32,544]{3,2,1,0:T(8,128)} %get-tuple-element.31, f32[11,4,32,544]{3,2,1,0:T(8,128)} %get-tuple-element.28, f32[11,2,32,544]{3,2,1,0:T(8,128)S(1)} %copy-done.2), kind=kLoop, calls=%fused_computation.5 | loop fusion | flops 11976704 | bytes 10305536 | tf_op jit(solution)/shard_map/correlate/reduce_sum | solution.py:111
  111.1 1.2 pad_maximum_fusion
  112.3 0.6 dynamic-slice.5
  112.9 48.1 %all-reduce.3.cloned.1.call-done = f32[2,4,2,32,544]{4,3,2,1,0:T(8,128)} async-done(((f32[2,4,2,32,544]{4,3,2,1,0:T(8,128)}), f32[2,4,2,32,544]{4,3,2,1,0:T(8,128)}) %all-reduce.3.cloned.1.call-update) | async-done | bytes 1114128
  161.0 2.6 %fusion.14 = f32[2,4,544,64]{2,3,1,0:T(8,128)S(1)} fusion(f32[64,32,1,1]{0,1,3,2:T(8,128)S(1)} %copy-done.7, f32[2,4,2,32,544]{4,3,2,1,0:T(8,128)} %all-reduce.3.cloned.1.call-done, u32[]{:T(128)} %bitcast.40), kind=kOutput, calls=%fused_computation.33 | convolution fusion | flops 53477376 | bytes 1778176 | tf_op jit(solution)/shard_map/inverse_scores/xp,srnpq->srnxq/dot_general | solution.py:118
  163.6 0.9 fusion.4
  164.6 1.1 fusion.11
  165.7 0.4 collective-permute-start
  166.1 3.2 %collective-permute-done = f32[1,4,1]{1,2,0:T(1,128)S(1)} collective-permute-done((f32[1,4,1]{1,2,0:T(1,128)S(1)}, f32[1,4,1]{1,2,0:T(1,128)S(1)}, u32[]{:S(2)}, u32[]{:S(2)}) %collective-permute-start) | collective-permute-done | bytes 48 | tf_op jit(solution)/shard_map/ppermute | solution.py:25
  169.4 1.1 collective-permute-done.1
  170.5 1.5 collective-permute-start.2
  172.1 2.1 %collective-permute-done.2 = f32[4,4,1]{1,2,0:T(1,128)S(1)} collective-permute-done((f32[4,4,1]{1,2,0:T(1,128)S(1)}, f32[4,4,1]{1,2,0:T(1,128)S(1)}, u32[]{:S(2)}, u32[]{:S(2)}) %collective-permute-start.2) | collective-permute-done | bytes 96 | tf_op jit(solution)/shard_map/ppermute | solution.py:25
  174.2 1.5 collective-permute-start.3
  175.8 2.1 %collective-permute-done.3 = f32[8,4,1]{1,2,0:T(1,128)S(1)} collective-permute-done((f32[8,4,1]{1,2,0:T(1,128)S(1)}, f32[8,4,1]{1,2,0:T(1,128)S(1)}, u32[]{:S(2)}, u32[]{:S(2)}) %collective-permute-start.3) | collective-permute-done | bytes 160 | tf_op jit(solution)/shard_map/ppermute | solution.py:25
  177.9 0.1 copy.54
  178.0 0.1 copy.55
  178.1 0.1 pad_maximum_fusion.3
  178.1 2.4 %collective-permute-start.4 = (f32[16,4,1]{0,1,2:T(4,128)S(1)}, f32[16,4,1]{0,1,2:T(4,128)S(1)}, u32[]{:S(2)}, u32[]{:S(2)}) collective-permute-start(f32[16,4,1]{0,1,2:T(4,128)S(1)} %pad_maximum_fusion.3), channel_id=1, source_target_pairs={{0,16},{1,17},{2,18},{3,19},{4,20},{5,21},{6,22},{7,23},{8,24},{9,... | collective-permute-start | bytes 776 | tf_op jit(solution)/shard_map/ppermute | solution.py:25
  180.5 2.1 %collective-permute-done.4 = f32[16,4,1]{0,1,2:T(4,128)S(1)} collective-permute-done((f32[16,4,1]{0,1,2:T(4,128)S(1)}, f32[16,4,1]{0,1,2:T(4,128)S(1)}, u32[]{:S(2)}, u32[]{:S(2)}) %collective-permute-start.4) | collective-permute-done | bytes 288 | tf_op jit(solution)/shard_map/ppermute | solution.py:25
  182.6 0.1 fusion.36
  182.8 0.1 pad_maximum_fusion.4
  182.8 0.1 dynamic-slice_bitcast_fusion.2
  182.9 0.7 copy.56
  183.6 0.5 reduce_max.29
  (53 shorter events, 0.3 us)
Async XLA Ops:
  7.2 56.1 %all-gather.2.cloned.1.call-start = ((), (), s32[]{:S(2)}) async-start(), calls=%async_computation | async-start | bytes 3063808 | tf_op jit(solution)/shard_map/all_gather | solution.py:130
  7.9 153.1 %all-reduce.3.cloned.1.call-start = ((), (), s32[]{:S(2)}) async-start(), calls=%async_computation.1 | async-start | bytes 2621440
  23.3 8.0 %copy-start.10 = (f32[16,32]{1,0:T(8,128)S(1)}, f32[16,32]{1,0:T(8,128)}, u32[]{:S(2)}) copy-start(f32[16,32]{1,0:T(8,128)} %constant.54.clone) | copy-start | bytes 6148
  23.3 8.0 %copy-start.11 = (f32[16,32]{1,0:T(8,128)S(1)}, f32[16,32]{1,0:T(8,128)}, u32[]{:S(2)}) copy-start(f32[16,32]{1,0:T(8,128)} %constant.55.clone) | copy-start | bytes 6148
  23.3 8.0 %copy-start.12 = (f32[16,17]{1,0:T(8,128)S(1)}, f32[16,17]{1,0:T(8,128)}, u32[]{:S(2)}) copy-start(f32[16,17]{1,0:T(8,128)} %constant.56.clone) | copy-start | bytes 3268
  23.3 8.0 %copy-start.13 = (f32[16,17]{1,0:T(8,128)S(1)}, f32[16,17]{1,0:T(8,128)}, u32[]{:S(2)}) copy-start(f32[16,17]{1,0:T(8,128)} %constant.57.clone) | copy-start | bytes 3268
  45.4 5.1 %copy-start.14 = (s32[3,2,256]{2,1,0:T(2,128)S(1)}, s32[3,2,256]{2,1,0:T(2,128)}, u32[]{:S(2)}) copy-start(s32[3,2,256]{2,1,0:T(2,128)} %param.19) | copy-start | bytes 18436
  45.4 5.1 %copy-start.17 = (f32[11,256]{1,0:T(8,128)S(1)}, f32[11,256]{1,0:T(8,128)}, u32[]{:S(2)}) copy-start(f32[11,256]{1,0:T(8,128)} %param.18) | copy-start | bytes 33796
  45.4 5.1 %copy-start.18 = (f32[11]{0:T(128)S(1)}, f32[11]{0:T(128)}, u32[]{:S(2)}) copy-start(f32[11]{0:T(128)} %param.17) | copy-start | bytes 136
  50.5 7.1 %copy-start.8 = (f32[64,16,1,1]{0,1,3,2:T(8,128)S(1)}, f32[64,16,1,1]{0,1,3,2:T(8,128)}, u32[]{:S(2)}) copy-start(f32[64,16,1,1]{0,1,3,2:T(8,128)} %constant.69) | copy-start | bytes 12292
  60.8 2.4 %copy-start.6 = (bf16[1024,544]{0,1:T(8,128)(2,1)S(1)}, bf16[1024,544]{0,1:T(8,128)(2,1)}, u32[]{:S(2)}) copy-start(bf16[1024,544]{0,1:T(8,128)(2,1)} %get-tuple-element.12) | copy-start | bytes 3342340
  63.3 3.9 %copy-start.5 = (bf16[1024,544]{0,1:T(8,128)(2,1)S(1)}, bf16[1024,544]{0,1:T(8,128)(2,1)}, u32[]{:S(2)}) copy-start(bf16[1024,544]{0,1:T(8,128)(2,1)} %get-tuple-element.13) | copy-start | bytes 3342340
  63.3 3.9 %copy-start.15 = (bf16[11,128,1024]{2,1,0:T(8,128)(2,1)S(1)}, bf16[11,128,1024]{2,1,0:T(8,128)(2,1)}, u32[]{:S(2)}) copy-start(bf16[11,128,1024]{2,1,0:T(8,128)(2,1)} %all-gather.2.cloned.1.call-done) | copy-start | bytes 8650756
  70.7 4.9 %copy-start.4 = (bf16[1024,544]{0,1:T(8,128)(2,1)S(1)}, bf16[1024,544]{0,1:T(8,128)(2,1)}, u32[]{:S(2)}) copy-start(bf16[1024,544]{0,1:T(8,128)(2,1)} %get-tuple-element.14) | copy-start | bytes 3342340
  75.6 3.9 %copy-start.3 = (bf16[1024,544]{0,1:T(8,128)(2,1)S(1)}, bf16[1024,544]{0,1:T(8,128)(2,1)}, u32[]{:S(2)}) copy-start(bf16[1024,544]{0,1:T(8,128)(2,1)} %get-tuple-element.15) | copy-start | bytes 3342340
  75.6 3.9 %copy-start.16 = (bf16[11,128,1024]{2,1,0:T(8,128)(2,1)S(1)}, bf16[11,128,1024]{2,1,0:T(8,128)(2,1)}, u32[]{:S(2)}) copy-start(bf16[11,128,1024]{2,1,0:T(8,128)(2,1)} %all-gather.2.cloned.1.call-done) | copy-start | bytes 8650756
  83.1 4.8 %copy-start.7 = (f32[64,32,1,1]{0,1,3,2:T(8,128)S(1)}, f32[64,32,1,1]{0,1,3,2:T(8,128)}, u32[]{:S(2)}) copy-start(f32[64,32,1,1]{0,1,3,2:T(8,128)} %constant.70) | copy-start | bytes 24580
  87.9 5.2 %copy-start.1 = (f32[1408,544]{1,0:T(8,128)S(1)}, f32[1408,544]{1,0:T(8,128)}, u32[]{:S(2)}) copy-start(f32[1408,544]{1,0:T(8,128)} %copy.51) | copy-start | bytes 9191428
  98.1 7.8 %copy-start.2 = (f32[11,2,32,544]{3,2,1,0:T(8,128)S(1)}, f32[11,2,32,544]{3,2,1,0:T(8,128)}, u32[]{:S(2)}) copy-start(f32[11,2,32,544]{3,2,1,0:T(8,128)} %get-tuple-element.30) | copy-start | bytes 4595716
  111.1 1.3 copy-start.19
  111.1 52.6 %copy-start.9 = (f32[544]{0:T(1024)S(1)}, f32[544]{0:T(1024)}, u32[]{:S(2)}) copy-start(f32[544]{0:T(1024)} %constant.60.clone) | copy-start | bytes 6532
  161.0 3.6 %copy-start = (f32[1024,544]{0,1:T(8,128)S(1)}, f32[1024,544]{0,1:T(8,128)}, u32[]{:S(2)}) copy-start(f32[1024,544]{0,1:T(8,128)} %sub.49) | copy-start | bytes 6684676
  165.7 3.6 %collective-permute-start = (f32[1,4,1]{1,2,0:T(1,128)S(1)}, f32[1,4,1]{1,2,0:T(1,128)S(1)}, u32[]{:S(2)}, u32[]{:S(2)}) collective-permute-start(f32[1,4,1]{1,2,0:T(1,128)S(1)} %bitcast.113), channel_id=1, source_target_pairs={{0,1},{1,0},{2,3},{3,2},{4,5},{5,4},{6,7},{7,6},{8,9},{9,8},{10,11... | collective-permute-start | bytes 56 | tf_op jit(solution)/shard_map/ppermute | solution.py:25
  169.3 1.2 collective-permute-start.1
  170.5 3.6 %collective-permute-start.2 = (f32[4,4,1]{1,2,0:T(1,128)S(1)}, f32[4,4,1]{1,2,0:T(1,128)S(1)}, u32[]{:S(2)}, u32[]{:S(2)}) collective-permute-start(f32[4,4,1]{1,2,0:T(1,128)S(1)} %pad_maximum_fusion.2), channel_id=1, source_target_pairs={{0,4},{1,5},{2,6},{3,7},{4,0},{5,1},{6,2},{7,3},{8,12},{9,13},{10,... | collective-permute-start | bytes 200 | tf_op jit(solution)/shard_map/ppermute | solution.py:25
  174.2 3.7 %collective-permute-start.3 = (f32[8,4,1]{1,2,0:T(1,128)S(1)}, f32[8,4,1]{1,2,0:T(1,128)S(1)}, u32[]{:S(2)}, u32[]{:S(2)}) collective-permute-start(f32[8,4,1]{1,2,0:T(1,128)S(1)} %pad_maximum_fusion.1), channel_id=1, source_target_pairs={{0,8},{1,9},{2,10},{3,11},{4,12},{5,13},{6,14},{7,15},{8,0},{9,1},... | collective-permute-start | bytes 392 | tf_op jit(solution)/shard_map/ppermute | solution.py:25
  178.1 4.5 %collective-permute-start.4 = (f32[16,4,1]{0,1,2:T(4,128)S(1)}, f32[16,4,1]{0,1,2:T(4,128)S(1)}, u32[]{:S(2)}, u32[]{:S(2)}) collective-permute-start(f32[16,4,1]{0,1,2:T(4,128)S(1)} %pad_maximum_fusion.3), channel_id=1, source_target_pairs={{0,16},{1,17},{2,18},{3,19},{4,20},{5,21},{6,22},{7,23},{8,24},{9,... | collective-permute-start | bytes 776 | tf_op jit(solution)/shard_map/ppermute | solution.py:25
Sparse Core Ops, SparseCore 0:
  10.2 47.0 all-gather.1
  112.4 48.5 all-reduce.2
